TPU v7x, 32 devices: a whole 2x2x4 slice. The times are simulated.
32 devices in a mesh: blk: 16 (over z, y, x), band: 2 (over core).
Axes of the slice: x: 2, y: 2, z: 4, core: 2. Of those that a mesh axis runs over, the one named last changes fastest.
Arguments:
- traces: bfloat16 [1024, 2, 8192], P('blk', None, 'band'), may hold values from -80 to 80
- sources: bfloat16 [32, 2, 8192], P('blk', None, 'band'), may hold values from -80 to 80
- owner: int32 [1024, 1], P('blk'), may hold values from 0 to 15; in each aligned block of 64 rows (0 to 63, 64 to 127, ...) at most 8 rows name the same one
Outputs:
- gathers: float32 [32, 4, 128, 256], P('blk', None, 'band')
Inputs may be any that keep to these rules, and one draw needn't show every extreme that they name: Among the 64 stations of one device's rows, at most 8 name the same owner block, and some owner block is named by exactly 8 of them in every draw.
All inputs are finite; a program needn't handle non-finite values.
Results may differ from a plain program's by a relative error of at most 0.017.
Values may be sent and summed in bfloat16 or wider, within the bound.
No kernel may reach another device: no remote copies, remote signals or barrier semaphores. Data moves between devices by JAX's collectives and lax.ppermute only.
A program may use at most 128 MiB of HBM per device.

v0:
```python
import math
import jax
import jax.numpy as jnp
from jax import lax
from jax.sharding import PartitionSpec as P

BINS = 8192
LAGS = 2048
DEC = 8
PERIOD = BINS // DEC
EPS = 1e-06


def per_device(traces, sources, owner):
    blocks = lax.axis_size("blk")
    station_count = traces.shape[0]
    source_count = sources.shape[0]
    group_bins = traces.shape[2]
    folds = group_bins // PERIOD
    capacity = max(2, 2 * station_count // blocks)
    lags_out = LAGS // DEC
    offsets = blocks // 4
    all_sources = lax.all_gather(sources, "blk", axis=0, tiled=True)
    trace_float = traces.astype(jnp.float32)
    all_source_float = all_sources.astype(jnp.float32)
    trace_power, source_power = lax.psum(
        (
            jnp.sum(trace_float * trace_float, axis=(1, 2)),
            jnp.sum(all_source_float * all_source_float, axis=(1, 2)),
        ),
        "band",
    )
    white_traces = (
        (trace_float * lax.rsqrt(trace_power / (2 * BINS) + EPS)[:, None, None])
        .astype(jnp.bfloat16)
        .reshape(station_count, 2 * group_bins)
    )
    white_sources = (
        (all_source_float * lax.rsqrt(source_power / (2 * BINS) + EPS)[:, None, None])
        .astype(jnp.bfloat16)
        .astype(jnp.float32)
        .reshape(blocks, source_count, 2, folds, PERIOD)
    )
    owners = owner[:, 0]
    owner_hits = (owners[:, None] == jnp.arange(blocks, dtype=jnp.int32)[None, :]).astype(jnp.int32)
    earlier = jnp.cumsum(owner_hits, axis=0) - owner_hits
    arrival = jnp.sum(owner_hits * earlier, axis=1)
    slot_index = owners * capacity + arrival
    placing = (
        jnp.arange(blocks * capacity, dtype=jnp.int32)[:, None] == slot_index[None, :]
    ).astype(jnp.bfloat16)
    placed = jnp.dot(placing, white_traces, preferred_element_type=jnp.float32)
    placed = placed.reshape(blocks, capacity, 2, folds, PERIOD)
    bin_index = jnp.arange(PERIOD, dtype=jnp.int32)
    lag_value = (jnp.arange(lags_out, dtype=jnp.int32) - lags_out // 2) * DEC
    phase_angle = jnp.mod(bin_index[:, None] * lag_value[None, :], BINS).astype(jnp.float32) * (
        2.0 * math.pi / BINS
    )
    table = jnp.concatenate([jnp.cos(phase_angle), jnp.sin(phase_angle)], axis=0).astype(
        jnp.bfloat16
    )
    norm_scale = BINS ** (-0.5)
    real_s = white_sources[:, None, :, 0]
    imag_s = white_sources[:, None, :, 1]
    cross = []
    for offset in range(offsets):
        visiting = jnp.roll(placed, offset, axis=0)
        real_t = visiting[:, :, None, 0]
        imag_t = visiting[:, :, None, 1]
        even = jnp.sum(real_t * real_s + imag_t * imag_s, axis=3)
        odd = jnp.sum(real_t * imag_s - imag_t * real_s, axis=3)
        cross.append(jnp.concatenate([even, odd], axis=-1))
    cross = jnp.stack(cross, axis=1).astype(jnp.bfloat16)
    rows = blocks * offsets * capacity * source_count
    partial = jnp.dot(cross.reshape(rows, 2 * PERIOD), table, preferred_element_type=jnp.float32)
    partial = (partial * norm_scale).astype(jnp.bfloat16)
    partial = partial.reshape(blocks, offsets, capacity, source_count, lags_out)
    arrived = lax.all_to_all(partial, "blk", split_axis=0, concat_axis=0, tiled=True)
    summed = lax.psum_scatter(arrived.astype(jnp.float32), "band", scatter_dimension=0, tiled=True)
    half = summed.shape[0]
    return jnp.transpose(summed, (3, 1, 0, 2, 4)).reshape(
        source_count, offsets, half * capacity, lags_out
    )


def solution(mesh):
    placed = (P("blk", None, "band"), P("blk", None, "band"), P("blk", None))
    return jax.shard_map(
        per_device,
        mesh=mesh,
        in_specs=placed,
        out_specs=P("blk", None, "band", None),
        check_vma=False,
    )
```

profile of v0, /device:TPU:0, one launch (start us, length us, event | category | flops | bytes accessed | tf_op | source)
XLA Modules:
  0.0 150.7 jit_solution(14130566093052021480)
XLA Ops:
  6.5 0.0 copy-start.8
  6.5 0.0 reduce-scatter.2.cloned.1.call-start
  6.5 45.7 %all_gather.3 = bf16[32,2,4096]{2,1,0:T(2,128)(2,1)S(1)} all-gather(bf16[2,2,4096]{2,1,0:T(2,128)(2,1)} %param.4), channel_id=1, replica_groups=mesh['blk'=16,'band'=2] {'blk'}, dimensions={0}, use_global_device_ids=true | all-gather | bytes 557056 | tf_op jit(solution)/shard_map/all_gather | solution.py:23
  52.2 0.0 copy-start.4
  52.2 0.8 copy-done.4
  53.0 0.8 fusion.12
  53.8 2.8 %fusion = f32[64]{0:T(128)S(1)} fusion(bf16[64,2,4096]{2,1,0:T(2,128)(2,1)} %param.3), kind=kLoop, calls=%fused_computation.17 | loop fusion | flops 1572800 | bytes 1048832 | tf_op jit(solution)/shard_map/reduce_sum | solution.py:28
  56.6 2.5 %all-reduce = (f32[32]{0:T(128)S(1)}, f32[64]{0:T(128)S(1)}) all-reduce(f32[32]{0:T(128)S(1)} %fusion.12, f32[64]{0:T(128)S(1)} %fusion), channel_id=1, replica_groups=mesh['blk'=16,'band'=2] {'band'}, use_global_device_ids=true, to_apply=%region_5.6 | all-reduce | flops 96 | bytes 768 | tf_op jit(solution)/shard_map/psum | solution.py:26
  59.1 2.5 %fusion.1 = bf16[64,2,4096]{2,1,0:T(2,128)(2,1)S(1)} fusion(bf16[64,2,4096]{2,1,0:T(2,128)(2,1)} %param.3, f32[64]{0:T(128)S(1)} %add_rsqrt_fusion.1), kind=kLoop, calls=%fused_computation.18 | loop fusion | flops 1572864 | bytes 2097408 | tf_op jit(solution)/shard_map/convert_element_type | solution.py:35
  61.6 0.6 copy.44
  62.2 0.0 copy-done.8
  62.2 0.1 fusion.26
  62.3 0.1 reduce_window_sum.11
  62.4 0.2 select_reduce_fusion
  62.6 0.7 fusion.24
  63.3 0.2 slice.107
  63.5 0.9 slice.106
  64.5 2.1 %slice.103 = f32[112,8192]{1,0:T(8,128)} slice(f32[128,8192]{1,0:T(8,128)S(1)} %fusion.24), slice={[0:112], [0:8192]} | slice | bytes 7340032 | tf_op jit(solution)/shard_map/jit(_roll_static)/slice | solution.py:67
  66.6 0.8 slice.102
  67.4 2.1 %slice.99 = f32[120,8192]{1,0:T(8,128)} slice(f32[128,8192]{1,0:T(8,128)S(1)} %fusion.24), slice={[0:120], [0:8192]} | slice | bytes 7864320 | tf_op jit(solution)/shard_map/jit(_roll_static)/slice | solution.py:67
  69.6 0.7 slice.98
  70.3 0.0 copy-start.5
  70.3 2.4 %slice_bitcast_fusion.1 = (f32[16,8,4,1024]{3,1,2,0:T(8,128)}, f32[16,8,4,1024]{3,1,2,0:T(8,128)}) fusion(f32[16,8,2,4,1024]{4,1,3,2,0:T(8,128)S(1)} %bitcast.46), kind=kLoop, calls=%fused_computation.32 | loop fusion | bytes 8388608 | tf_op jit(solution)/shard_map/mul | solution.py:70
  72.7 0.0 copy-done.5
  72.7 1.5 %fusion.23 = f32[32,2,4096]{2,1,0:T(2,128)} fusion(f32[32]{0:T(128)S(1)} %add_rsqrt_fusion, bf16[32,2,4096]{2,1,0:T(2,128)(2,1)S(1)} %copy-done.5), kind=kLoop, calls=%fused_computation.57 | loop fusion | flops 1048576 | bytes 1572992 | tf_op jit(solution)/shard_map/reshape | solution.py:42
  74.2 3.3 %reshape.51 = f32[16,2,2,4,1024]{4,3,2,1,0:T(4,128)} reshape(f32[32,2,4096]{2,1,0:T(2,128)} %fusion.23) | data formatting | bytes 2097152 | tf_op jit(solution)/shard_map/reshape | solution.py:42
  77.6 1.3 slice_bitcast_fusion.3
  78.9 0.0 copy-start.1
  78.9 0.0 copy-start.6
  78.9 1.6 %fusion.3 = (f32[16,8,4,1024]{3,1,2,0:T(8,128)S(1)}, f32[16,8,4,1024]{3,1,2,0:T(8,128)S(1)}) fusion(f32[3,8,2,4,1024]{4,1,3,2,0:T(8,128)} %bitcast.52, f32[13,8,2,4,1024]{4,1,3,2,0:T(8,128)S(1)} %bitcast.49), kind=kLoop, calls=%fused_computation.20 | loop fusion | flops 1048576 | bytes 8388608 | tf_op jit(solution)/shard_map/mul | solution.py:70
  80.5 0.6 copy-done.1
  81.2 0.1 copy-done.6
  81.3 0.0 copy-start
  81.3 0.0 copy-start.7
  81.3 0.5 fusion.5
  81.8 1.6 %copy-done = f32[120,8192]{1,0:T(8,128)S(1)} copy-done((f32[120,8192]{1,0:T(8,128)S(1)}, f32[120,8192]{1,0:T(8,128)}, u32[]{:S(2)}) %copy-start) | copy-done | bytes 3932184
  83.4 0.0 copy-done.7
  83.4 0.0 copy-start.2
  83.4 0.0 copy-start.3
  83.4 0.5 fusion.7
  83.9 1.1 copy-done.2
  85.0 0.6 copy-done.3
  85.6 7.3 %add_reduce_fusion.3 = (bf16[16,8,2,1024]{3,1,2,0:T(8,128)(2,1)S(1)}, bf16[16,8,2,1024]{3,1,2,0:T(8,128)(2,1)S(1)}, bf16[16,8,2,1024]{3,1,2,0:T(8,128)(2,1)S(1)}...) fusion(f32[16,2,4,1024]{3,2,1,0:T(4,128)S(1)} %get-tuple-elemen, ...), kind=kLoop, calls=%fused_computation.14 | loop fusion | flops 31457280 | bytes 22020096 | tf_op jit(solution)/shard_map/reduce_sum | solution.py:70
  92.9 0.2 maximum_bitcast_fusion
  93.1 0.2 maximum_bitcast_fusion.2
  93.3 0.6 pad_maximum_fusion
  93.9 6.3 %copy.41 = bf16[16,4,8,2,2048]{4,3,2,1,0:T(2,128)(2,1)} copy(bf16[16,4,8,2,2048]{4,2,3,0,1:T(8,128)(2,1)S(1)} %pad_maximum_fusion) | data formatting | bytes 8388608 | tf_op jit(solution)/shard_map/stack | solution.py:73
  100.2 7.2 %convert_element_type.39 = bf16[1024,2048]{1,0:T(8,128)(2,1)} reshape(bf16[16,4,8,2,2048]{4,3,2,1,0:T(2,128)(2,1)} %copy.41) | data formatting | bytes 8388608 | tf_op jit(solution)/shard_map/convert_element_type | solution.py:73
  107.4 4.4 %cosine_convert_fusion = (bf16[1024,256]{1,0:T(8,128)(2,1)S(1)}, bf16[1024,256]{1,0:T(8,128)(2,1)S(1)}) fusion(s32[256]{0:T(256)S(1)} %add_multiply_fusion), kind=kLoop, calls=%fused_computation.53 | loop fusion | flops 4194304 | bytes 1049600 | tf_op jit(solution)/shard_map/convert.1
  111.8 3.4 %fusion.11 = bf16[1024,256]{1,0:T(8,128)(2,1)S(1)} fusion(bf16[1024,2048]{1,0:T(8,128)(2,1)} %convert_element_type.39, bf16[1024,256]{1,0:T(8,128)(2,1)S(1)} %get-tuple-element.32, bf16[1024,256]{1,0:T(8,128)(2,1)S(1)} %get-tuple-element.31), kind=kOutput, calls=%fused_computation.39 | convolution fusion | flops 1076363264 | bytes 5767168 | tf_op jit(solution)/shard_map/dot_general | solution.py:75
  115.2 0.2 reshape.48
  115.4 0.1 copy.42
  115.5 18.1 %all_to_all.5 = bf16[16,4,8,2,256]{4,2,3,1,0:T(8,128)(2,1)S(1)} all-to-all(bf16[16,4,8,2,256]{4,2,3,1,0:T(8,128)(2,1)S(1)} %copy.42), channel_id=1, replica_groups=mesh['blk'=16,'band'=2] {'blk'}, dimensions={0} | all-to-all | bytes 1048576 | tf_op jit(solution)/shard_map/all_to_all | solution.py:78
  133.6 1.1 convert_element_type.42
  134.7 0.0 reduce-scatter.2.cloned.1.call-update
  134.8 7.2 %reduce-scatter.2.cloned.1.call-done = f32[8,4,8,2,256]{4,2,3,1,0:T(8,128)} async-done(((f32[16,4,8,2,256]{4,2,3,1,0:T(8,128)}), f32[8,4,8,2,256]{4,2,3,1,0:T(8,128)}) %reduce-scatter.2.cloned.1.call-update) | async-done | bytes 524304 | tf_op jit(solution)/shard_map/reduce_scatter | solution.py:79
  142.0 1.9 %copy.46 = f32[8,4,8,2,256]{4,2,0,1,3:T(8,128)} copy(f32[8,4,8,2,256]{4,2,3,1,0:T(8,128)} %reduce-scatter.2.cloned.1.call-done) | data formatting | bytes 1048576 | tf_op jit(solution)/shard_map/reduce_scatter | solution.py:79
  (4 shorter events, 0.0 us)
Async XLA Ops:
  6.5 55.7 %copy-start.8 = (s32[64,1]{0,1:T(1,128)S(1)}, s32[64,1]{0,1:T(1,128)}, u32[]{:S(2)}) copy-start(s32[64,1]{0,1:T(1,128)} %param.5) | copy-start | bytes 772
  6.5 135.4 %reduce-scatter.2.cloned.1.call-start = ((), (), s32[]{:S(2)}) async-start(), calls=%async_computation.2 | async-start | bytes 1572864 | tf_op jit(solution)/shard_map/reduce_scatter | solution.py:79
  52.2 0.8 copy-start.4
  70.3 2.4 %copy-start.5 = (bf16[32,2,4096]{2,1,0:T(2,128)(2,1)S(1)}, bf16[32,2,4096]{2,1,0:T(2,128)(2,1)}, u32[]{:S(2)}) copy-start(bf16[32,2,4096]{2,1,0:T(2,128)(2,1)} %copy-done.4) | copy-start | bytes 1572868
  78.9 2.3 %copy-start.1 = (f32[112,8192]{1,0:T(8,128)S(1)}, f32[112,8192]{1,0:T(8,128)}, u32[]{:S(2)}) copy-start(f32[112,8192]{1,0:T(8,128)} %slice.103) | copy-start | bytes 11010052
  78.9 2.4 %copy-start.6 = (f32[16,8192]{1,0:T(8,128)S(1)}, f32[16,8192]{1,0:T(8,128)}, u32[]{:S(2)}) copy-start(f32[16,8192]{1,0:T(8,128)} %slice.102) | copy-start | bytes 1572868
  81.3 2.1 %copy-start = (f32[120,8192]{1,0:T(8,128)S(1)}, f32[120,8192]{1,0:T(8,128)}, u32[]{:S(2)}) copy-start(f32[120,8192]{1,0:T(8,128)} %slice.99) | copy-start | bytes 11796484
  81.3 2.1 %copy-start.7 = (f32[8,8192]{1,0:T(8,128)S(1)}, f32[8,8192]{1,0:T(8,128)}, u32[]{:S(2)}) copy-start(f32[8,8192]{1,0:T(8,128)} %slice.98) | copy-start | bytes 786436
  83.4 1.6 %copy-start.2 = (f32[16,8,4,1024]{3,1,2,0:T(8,128)S(1)}, f32[16,8,4,1024]{3,1,2,0:T(8,128)}, u32[]{:S(2)}) copy-start(f32[16,8,4,1024]{3,1,2,0:T(8,128)} %get-tuple-element.27) | copy-start | bytes 6291460
  83.4 2.2 %copy-start.3 = (f32[16,8,4,1024]{3,1,2,0:T(8,128)S(1)}, f32[16,8,4,1024]{3,1,2,0:T(8,128)}, u32[]{:S(2)}) copy-start(f32[16,8,4,1024]{3,1,2,0:T(8,128)} %get-tuple-element.28) | copy-start | bytes 6291460
Sparse Core Ops, SparseCore 0:
  134.9 7.0 reduce-scatter.1
where the time goes:
time: 151 us
  blocking collectives  66.2 us (44%)
  local copies, waits for them, and re-layouts  35.1 us (23%)
  other arithmetic  24.5 us (16%)
  between operations  13.6 us (9%)
  waiting for transfers between devices  7.22 us (5%)
  matrix products  4.13 us (3%)
    all_gather x1, blocking collectives, per_device(): all_sources = lax.all_gather(sources, 'blk', axis=0, tiled=True)  45.7 us
    all_to_all x1, blocking collectives, per_device(): lax.all_to_all(partial, 'blk', split_axis=0, concat_axis=0, tiled=True)  18.1 us
    reduce_sum x1, other arithmetic, per_device(): even = jnp.sum(real_t * real_s + imag_t * imag_s, axis=3)  7.3 us
    reduce_scatter x1, waiting for transfers between devices, per_device(): lax.psum_scatter(arrived.astype(jnp.float32), 'band', scatter_dimension=0...  7.2 us
    convert_element_type x1, local copies, waits for them, and re-layouts, per_device(): cross = jnp.stack(cross, axis=1).astype(jnp.bfloat16)  7.2 us
    slice x6, local copies, waits for them, and re-layouts, per_device(): visiting = jnp.roll(placed, offset, axis=0)  6.99 us
    another operation x1, local copies, waits for them, and re-layouts, per_device(): cross = jnp.stack(cross, axis=1).astype(jnp.bfloat16)  6.3 us
    unnamed x19, local copies, waits for them, and re-layouts  5.42 us
  transfers between devices with their start and end apart: 1, of which 1 were waited for; matrix products, arithmetic and copies ran while one was open for 0% of the time, Pallas kernels for 0%

commit v1 on v0

--- a/solution.py
+++ b/solution.py
@@ -12,6 +12,29 @@
 
 
 def per_device(traces, sources, owner):
+
+    def recast_the_strips_all(net_axis, in_dim, s0):
+        outcome_arr, y1, block_out = (
+            lax.psum(1, net_axis),
+            lax.axis_index(net_axis),
+            s0.shape[in_dim],
+        )
+        passed, b_next = (s0, 1)
+        while b_next < outcome_arr:
+            passed = jnp.concatenate(
+                [
+                    passed,
+                    lax.ppermute(
+                        passed,
+                        net_axis,
+                        list(map(lambda b: (b, (b - b_next) % outcome_arr), range(outcome_arr))),
+                    ),
+                ],
+                axis=in_dim,
+            )
+            b_next = 2 * b_next
+        return jnp.roll(passed, y1 * block_out, axis=in_dim)
+
     blocks = lax.axis_size("blk")
     station_count = traces.shape[0]
     source_count = sources.shape[0]
@@ -20,7 +43,7 @@
     capacity = max(2, 2 * station_count // blocks)
     lags_out = LAGS // DEC
     offsets = blocks // 4
-    all_sources = lax.all_gather(sources, "blk", axis=0, tiled=True)
+    all_sources = recast_the_strips_all("blk", 0, sources)
     trace_float = traces.astype(jnp.float32)
     all_source_float = all_sources.astype(jnp.float32)
     trace_power, source_power = lax.psum(

time: 151 us -> 140 us (0.927)
  blocking collectives: 66.2 us -> 22.7 us
  waiting for transfers between devices: 7.22 us -> 26.7 us
  starting transfers between devices: 0.01 us -> 8.07 us
  other arithmetic: 24.5 us -> 27.1 us
  local copies, waits for them, and re-layouts: 35.1 us -> 37.2 us
    all_gather x1 -> x0, blocking collectives: 45.7 us -> none  [per_device(): all_sources = lax.all_gather(sources, 'blk', axis=0, tiled=True)]
    ppermute x0 -> x4, waiting for transfers between devices: none -> 19.7 us  [recast_the_strips_all(): lax.ppermute(passed, net_axis, list(map(lambda b: (b, (b - b_next) % outc...]
    ppermute x0 -> x4, starting transfers between devices: none -> 8.06 us  [recast_the_strips_all(): lax.ppermute(passed, net_axis, list(map(lambda b: (b, (b - b_next) % outc...]
    concatenate x0 -> x3, other arithmetic: none -> 2.91 us  [recast_the_strips_all(): jnp.concatenate([passed, lax.ppermute(passed, net_axis, list(map(lambda b...]
    all_to_all x1, blocking collectives: 18.1 us -> 20.1 us  [per_device(): lax.all_to_all(partial, 'blk', split_axis=0, concat_axis=0, tiled=True)]
    mul x3, other arithmetic: 2.66 us -> 0.92 us  [per_device(): even = jnp.sum(real_t * real_s + imag_t * imag_s, axis=3)]
    unnamed x19 -> x34, local copies, waits for them, and re-layouts: 5.42 us -> 6.19 us
  transfers between devices with their start and end apart: 1 -> 5, of which waited for: 1 -> 4; matrix products, arithmetic and copies ran while one was open for 0% -> 8% of each run, Pallas kernels for 0% -> 0%
where the time goes in v1:
time: 140 us; the launch traced here: 139 us
  local copies, waits for them, and re-layouts  37.2 us (27%)
  other arithmetic  27.1 us (19%)
  waiting for transfers between devices  26.7 us (19%)
  blocking collectives  22.7 us (16%)
  between operations  13.6 us (10%)
  starting transfers between devices  8.07 us (6%)
  matrix products  4.12 us (3%)
    all_to_all x1, blocking collectives, per_device(): lax.all_to_all(partial, 'blk', split_axis=0, concat_axis=0, tiled=True)  20.1 us
    ppermute x4, waiting for transfers between devices, recast_the_strips_all(): lax.ppermute(passed, net_axis, list(map(lambda b: (b, (b - b_next) % outc...  19.7 us
    ppermute x4, starting transfers between devices, recast_the_strips_all(): lax.ppermute(passed, net_axis, list(map(lambda b: (b, (b - b_next) % outc...  8.06 us
    slice x6, local copies, waits for them, and re-layouts, per_device(): visiting = jnp.roll(placed, offset, axis=0)  7.36 us
    reduce_sum x1, other arithmetic, per_device(): even = jnp.sum(real_t * real_s + imag_t * imag_s, axis=3)  7.35 us
    convert_element_type x1, local copies, waits for them, and re-layouts, per_device(): cross = jnp.stack(cross, axis=1).astype(jnp.bfloat16)  7.3 us
    reduce_scatter x1, waiting for transfers between devices, per_device(): lax.psum_scatter(arrived.astype(jnp.float32), 'band', scatter_dimension=0...  7.01 us
    another operation x1, local copies, waits for them, and re-layouts, per_device(): cross = jnp.stack(cross, axis=1).astype(jnp.bfloat16)  6.34 us
  transfers between devices with their start and end apart: 5, of which 4 were waited for; matrix products, arithmetic and copies ran while one was open for 8% of the time, Pallas kernels for 0%

profile of v1, /device:TPU:0, one launch (start us, length us, event | category | flops | bytes accessed | tf_op | source)
XLA Modules:
  0.0 139.4 jit_solution(5224378693188938661)
XLA Ops:
  6.5 0.0 reduce-scatter.2.cloned.1.call-start
  6.5 6.9 %collective-permute-start = (bf16[2,2,4096]{2,1,0:T(2,128)(2,1)}, bf16[2,2,4096]{2,1,0:T(2,128)(2,1)S(1)}, u32[]{:S(2)}, u32[]{:S(2)}) collective-permute-start(bf16[2,2,4096]{2,1,0:T(2,128)(2,1)} %param.4), channel_id=1, source_target_pairs={{0,30},{2,0},{4,2},{6,4},{8,6},{10,8},{12,10},{14,12},{16,14},{18,... | collective-permute-start | bytes 98312 | tf_op jit(solution)/shard_map/ppermute | solution.py:27
  13.5 0.8 constant_dynamic-update-slice_fusion.9
  14.3 2.8 %fusion = f32[64]{0:T(128)S(1)} fusion(bf16[64,2,4096]{2,1,0:T(2,128)(2,1)} %param.3), kind=kLoop, calls=%fused_computation.17 | loop fusion | flops 1572800 | bytes 1048832 | tf_op jit(solution)/shard_map/reduce_sum | solution.py:51
  17.1 0.7 fusion.26
  17.8 0.1 reduce_window_sum.11
  17.9 0.8 select_reduce_fusion
  18.8 5.0 %cosine_convert_fusion = (bf16[1024,256]{1,0:T(8,128)(2,1)}, bf16[1024,256]{1,0:T(8,128)(2,1)}) fusion(s32[256]{0:T(256)S(1)} %add_multiply_fusion), kind=kLoop, calls=%fused_computation.53 | loop fusion | flops 4194304 | bytes 1049600 | tf_op jit(solution)/shard_map/convert.1
  23.8 0.7 multiply_add_fusion
  24.5 0.0 collective-permute-done
  24.5 0.8 pad_maximum_fusion.6
  25.3 0.6 collective-permute-start.1
  25.9 3.7 %collective-permute-done.1 = bf16[4,2,4096]{2,1,0:T(2,128)(2,1)S(1)} collective-permute-done((bf16[4,2,4096]{2,1,0:T(2,128)(2,1)S(1)}, bf16[4,2,4096]{2,1,0:T(2,128)(2,1)S(1)}, u32[]{:S(2)}, u32[]{:S(2)}) %collective-permute-start.1) | collective-permute-done | bytes 65568 | tf_op jit(solution)/shard_map/ppermute | solution.py:27
  29.6 0.9 pad_maximum_fusion.5
  30.6 0.5 collective-permute-start.2
  31.1 0.1 constant_dynamic-update-slice_fusion.7
  31.1 4.5 %collective-permute-done.2 = bf16[8,2,4096]{2,1,0:T(2,128)(2,1)S(1)} collective-permute-done((bf16[8,2,4096]{2,1,0:T(2,128)(2,1)S(1)}, bf16[8,2,4096]{2,1,0:T(2,128)(2,1)S(1)}, u32[]{:S(2)}, u32[]{:S(2)}) %collective-permute-start.2) | collective-permute-done | bytes 131104 | tf_op jit(solution)/shard_map/ppermute | solution.py:27
  35.6 1.1 pad_maximum_fusion.4
  36.7 0.1 collective-permute-start.3
  36.8 0.1 constant_dynamic-update-slice_fusion.6
  36.9 11.5 %collective-permute-done.3 = bf16[16,2,4096]{2,1,0:T(2,128)(2,1)S(1)} collective-permute-done((bf16[16,2,4096]{2,1,0:T(2,128)(2,1)S(1)}, bf16[16,2,4096]{2,1,0:T(2,128)(2,1)S(1)}, u32[]{:S(2)}, u32[]{:S(2)}) %collective-permute-start.3) | collective-permute-done | bytes 262176 | tf_op jit(solution)/shard_map/ppermute | solution.py:27
  48.4 0.2 constant_dynamic-update-slice_fusion.5
  48.7 0.1 constant_dynamic-update-slice_fusion.2
  48.8 0.1 constant_dynamic-update-slice_fusion.1
  48.9 0.2 constant_dynamic-update-slice_fusion
  49.1 0.8 fusion.12
  49.9 2.6 %all-reduce = (f32[32]{0:T(128)S(1)}, f32[64]{0:T(128)S(1)}) all-reduce(f32[32]{0:T(128)S(1)} %fusion.12, f32[64]{0:T(128)S(1)} %fusion), channel_id=1, replica_groups=mesh['blk'=16,'band'=2] {'band'}, use_global_device_ids=true, to_apply=%region_5.6 | all-reduce | flops 96 | bytes 768 | tf_op jit(solution)/shard_map/psum | solution.py:49
  52.6 0.0 copy-done.3
  52.6 1.3 fusion.1
  53.9 0.6 copy.44
  54.5 0.7 fusion.24
  55.2 0.8 slice.98
  56.0 2.4 %slice.99 = f32[120,8192]{1,0:T(8,128)} slice(f32[128,8192]{1,0:T(8,128)S(1)} %fusion.24), slice={[0:120], [0:8192]} | slice | bytes 7864320 | tf_op jit(solution)/shard_map/jit(_roll_static)/slice | solution.py:90
  58.4 0.8 slice.102
  59.2 2.2 %slice.103 = f32[112,8192]{1,0:T(8,128)} slice(f32[128,8192]{1,0:T(8,128)S(1)} %fusion.24), slice={[0:112], [0:8192]} | slice | bytes 7340032 | tf_op jit(solution)/shard_map/jit(_roll_static)/slice | solution.py:90
  61.4 0.9 slice.106
  62.3 0.2 slice.107
  62.6 1.0 copy-done.7
  63.6 1.5 %fusion.23 = f32[32,2,4096]{2,1,0:T(2,128)} fusion(f32[32]{0:T(128)S(1)} %add_rsqrt_fusion, bf16[64,2,4096]{2,1,0:T(2,128)(2,1)S(1)} %copy-done.7, s32[]{:T(128)S(6)} %select_n.22), kind=kLoop, calls=%fused_computation.57 | loop fusion | flops 1048576 | bytes 1572996 | tf_op jit(solution)/shard_map/reshape | solution.py:65
  65.1 3.3 %reshape.51 = f32[16,2,2,4,1024]{4,3,2,1,0:T(4,128)} reshape(f32[32,2,4096]{2,1,0:T(2,128)} %fusion.23) | data formatting | bytes 2097152 | tf_op jit(solution)/shard_map/reshape | solution.py:65
  68.4 1.3 slice_bitcast_fusion.3
  69.8 2.9 %slice_bitcast_fusion.1 = (f32[16,8,4,1024]{3,1,2,0:T(8,128)S(1)}, f32[16,8,4,1024]{3,1,2,0:T(8,128)S(1)}) fusion(f32[16,8,2,4,1024]{4,1,3,2,0:T(8,128)} %bitcast.46), kind=kLoop, calls=%fused_computation.32 | loop fusion | bytes 8388608 | tf_op jit(solution)/shard_map/mul | solution.py:93
  72.7 0.4 copy-done.1
  73.1 0.0 copy-done.8
  73.2 0.3 fusion.7
  73.5 1.7 %copy-done.2 = f32[112,8192]{1,0:T(8,128)S(1)} copy-done((f32[112,8192]{1,0:T(8,128)S(1)}, f32[112,8192]{1,0:T(8,128)}, u32[]{:S(2)}) %copy-start.2) | copy-done | bytes 3670040
  75.2 0.1 copy-done.5
  75.3 0.3 fusion.5
  75.6 0.8 copy-done.4
  76.4 0.3 fusion.3
  76.7 7.3 %add_reduce_fusion.3 = (bf16[16,8,2,1024]{3,1,2,0:T(8,128)(2,1)S(1)}, bf16[16,8,2,1024]{3,1,2,0:T(8,128)(2,1)S(1)}, bf16[16,8,2,1024]{3,1,2,0:T(8,128)(2,1)S(1)}...) fusion(f32[16,2,4,1024]{3,2,1,0:T(4,128)S(1)} %get-tuple-elemen, ...), kind=kLoop, calls=%fused_computation.14 | loop fusion | flops 31457280 | bytes 22020096 | tf_op jit(solution)/shard_map/reduce_sum | solution.py:93
  84.1 0.2 maximum_bitcast_fusion.2
  84.3 0.2 maximum_bitcast_fusion
  84.5 0.6 pad_maximum_fusion
  85.1 6.3 %copy.41 = bf16[16,4,8,2,2048]{4,3,2,1,0:T(2,128)(2,1)} copy(bf16[16,4,8,2,2048]{4,2,3,0,1:T(8,128)(2,1)S(1)} %pad_maximum_fusion) | data formatting | bytes 8388608 | tf_op jit(solution)/shard_map/stack | solution.py:96
  91.4 7.3 %convert_element_type.39 = bf16[1024,2048]{1,0:T(8,128)(2,1)} reshape(bf16[16,4,8,2,2048]{4,3,2,1,0:T(2,128)(2,1)} %copy.41) | data formatting | bytes 8388608 | tf_op jit(solution)/shard_map/convert_element_type | solution.py:96
  98.7 3.4 %fusion.11 = bf16[1024,256]{1,0:T(8,128)(2,1)S(1)} fusion(bf16[1024,2048]{1,0:T(8,128)(2,1)} %convert_element_type.39, bf16[1024,256]{1,0:T(8,128)(2,1)S(1)} %copy-done.11, bf16[1024,256]{1,0:T(8,128)(2,1)S(1)} %copy-done.10), kind=kOutput, calls=%fused_computation.39 | convolution fusion | flops 1076363264 | bytes 5767168 | tf_op jit(solution)/shard_map/dot_general | solution.py:98
  102.2 0.2 reshape.48
  102.4 0.1 copy.42
  102.5 20.1 %all_to_all.5 = bf16[16,4,8,2,256]{4,2,3,1,0:T(8,128)(2,1)S(1)} all-to-all(bf16[16,4,8,2,256]{4,2,3,1,0:T(8,128)(2,1)S(1)} %copy.42), channel_id=1, replica_groups=mesh['blk'=16,'band'=2] {'blk'}, dimensions={0} | all-to-all | bytes 1048576 | tf_op jit(solution)/shard_map/all_to_all | solution.py:101
  122.6 1.1 convert_element_type.42
  123.7 0.0 reduce-scatter.2.cloned.1.call-update
  123.7 7.0 %reduce-scatter.2.cloned.1.call-done = f32[8,4,8,2,256]{4,2,3,1,0:T(8,128)} async-done(((f32[16,4,8,2,256]{4,2,3,1,0:T(8,128)}), f32[8,4,8,2,256]{4,2,3,1,0:T(8,128)}) %reduce-scatter.2.cloned.1.call-update) | async-done | bytes 524304 | tf_op jit(solution)/shard_map/reduce_scatter | solution.py:102
  130.7 1.9 %copy.46 = f32[8,4,8,2,256]{4,2,0,1,3:T(8,128)} copy(f32[8,4,8,2,256]{4,2,3,1,0:T(8,128)} %reduce-scatter.2.cloned.1.call-done) | data formatting | bytes 1048576 | tf_op jit(solution)/shard_map/reduce_scatter | solution.py:102
  (23 shorter events, 0.2 us)
Async XLA Ops:
  6.5 42.1 %copy-start.9 = (bf16[2,2,4096]{2,1,0:T(2,128)(2,1)S(1)}, bf16[2,2,4096]{2,1,0:T(2,128)(2,1)}, u32[]{:S(2)}) copy-start(bf16[2,2,4096]{2,1,0:T(2,128)(2,1)} %param.4) | copy-start | bytes 98308
  6.5 46.0 %copy-start.3 = (bf16[64,2,4096]{2,1,0:T(2,128)(2,1)S(1)}, bf16[64,2,4096]{2,1,0:T(2,128)(2,1)}, u32[]{:S(2)}) copy-start(bf16[64,2,4096]{2,1,0:T(2,128)(2,1)} %param.3) | copy-start | bytes 3145732
  6.5 124.2 %reduce-scatter.2.cloned.1.call-start = ((), (), s32[]{:S(2)}) async-start(), calls=%async_computation.2 | async-start | bytes 1572864 | tf_op jit(solution)/shard_map/reduce_scatter | solution.py:102
  6.5 17.9 %collective-permute-start = (bf16[2,2,4096]{2,1,0:T(2,128)(2,1)}, bf16[2,2,4096]{2,1,0:T(2,128)(2,1)S(1)}, u32[]{:S(2)}, u32[]{:S(2)}) collective-permute-start(bf16[2,2,4096]{2,1,0:T(2,128)(2,1)} %param.4), channel_id=1, source_target_pairs={{0,30},{2,0},{4,2},{6,4},{8,6},{10,8},{12,10},{14,12},{16,14},{18,... | collective-permute-start | bytes 98312 | tf_op jit(solution)/shard_map/ppermute | solution.py:27
  25.3 4.3 %collective-permute-start.1 = (bf16[4,2,4096]{2,1,0:T(2,128)(2,1)S(1)}, bf16[4,2,4096]{2,1,0:T(2,128)(2,1)S(1)}, u32[]{:S(2)}, u32[]{:S(2)}) collective-permute-start(bf16[4,2,4096]{2,1,0:T(2,128)(2,1)S(1)} %pad_maximum_fusion.6), channel_id=1, source_target_pairs={{0,28},{2,30},{4,0},{6,2},{8,4},{10,6},{12,8},{14,10},{16,12},{18,... | collective-permute-start | bytes 196616 | tf_op jit(solution)/shard_map/ppermute | solution.py:27
  30.6 5.0 %collective-permute-start.2 = (bf16[8,2,4096]{2,1,0:T(2,128)(2,1)S(1)}, bf16[8,2,4096]{2,1,0:T(2,128)(2,1)S(1)}, u32[]{:S(2)}, u32[]{:S(2)}) collective-permute-start(bf16[8,2,4096]{2,1,0:T(2,128)(2,1)S(1)} %pad_maximum_fusion.5), channel_id=1, source_target_pairs={{0,24},{2,26},{4,28},{6,30},{8,0},{10,2},{12,4},{14,6},{16,8},{18,... | collective-permute-start | bytes 393224 | tf_op jit(solution)/shard_map/ppermute | solution.py:27
  36.7 11.7 %collective-permute-start.3 = (bf16[16,2,4096]{2,1,0:T(2,128)(2,1)S(1)}, bf16[16,2,4096]{2,1,0:T(2,128)(2,1)S(1)}, u32[]{:S(2)}, u32[]{:S(2)}) collective-permute-start(bf16[16,2,4096]{2,1,0:T(2,128)(2,1)S(1)} %pad_maximum_fusion.4), channel_id=1, source_target_pairs={{0,16},{2,18},{4,20},{6,22},{8,24},{10,26},{12,28},{14,30},{16,0},... | collective-permute-start | bytes 786440 | tf_op jit(solution)/shard_map/ppermute | solution.py:27
  49.1 6.1 %copy-start.6 = (bf16[64,2,4096]{2,1,0:T(2,128)(2,1)}, bf16[64,2,4096]{2,1,0:T(2,128)(2,1)S(1)}, u32[]{:S(2)}) copy-start(bf16[64,2,4096]{2,1,0:T(2,128)(2,1)S(1)} %constant_dynamic-update-slice_fusion) | copy-start | bytes 3145732
  55.2 7.1 %copy-start = (f32[128,8192]{1,0:T(8,128)}, f32[128,8192]{1,0:T(8,128)S(1)}, u32[]{:S(2)}) copy-start(f32[128,8192]{1,0:T(8,128)S(1)} %fusion.24) | copy-start | bytes 12582916
  62.3 1.2 copy-start.7
  69.8 3.4 %copy-start.1 = (f32[120,8192]{1,0:T(8,128)S(1)}, f32[120,8192]{1,0:T(8,128)}, u32[]{:S(2)}) copy-start(f32[120,8192]{1,0:T(8,128)} %slice.99) | copy-start | bytes 11796484
  69.8 3.4 %copy-start.8 = (f32[8,8192]{1,0:T(8,128)S(1)}, f32[8,8192]{1,0:T(8,128)}, u32[]{:S(2)}) copy-start(f32[8,8192]{1,0:T(8,128)} %slice.98) | copy-start | bytes 786436
  73.2 2.0 %copy-start.2 = (f32[112,8192]{1,0:T(8,128)S(1)}, f32[112,8192]{1,0:T(8,128)}, u32[]{:S(2)}) copy-start(f32[112,8192]{1,0:T(8,128)} %slice.103) | copy-start | bytes 11010052
  73.2 2.1 %copy-start.5 = (f32[16,8192]{1,0:T(8,128)S(1)}, f32[16,8192]{1,0:T(8,128)}, u32[]{:S(2)}) copy-start(f32[16,8192]{1,0:T(8,128)} %slice.102) | copy-start | bytes 1572868
  75.3 1.1 copy-start.4
  91.4 7.3 %copy-start.10 = (bf16[1024,256]{1,0:T(8,128)(2,1)S(1)}, bf16[1024,256]{1,0:T(8,128)(2,1)}, u32[]{:S(2)}) copy-start(bf16[1024,256]{1,0:T(8,128)(2,1)} %get-tuple-element.31) | copy-start | bytes 1572868
  91.4 7.3 %copy-start.11 = (bf16[1024,256]{1,0:T(8,128)(2,1)S(1)}, bf16[1024,256]{1,0:T(8,128)(2,1)}, u32[]{:S(2)}) copy-start(bf16[1024,256]{1,0:T(8,128)(2,1)} %get-tuple-element.32) | copy-start | bytes 1572868
Sparse Core Ops, SparseCore 0:
  123.8 6.8 reduce-scatter.1
